TPU v7x, 128 devices: a whole 4x4x4 slice. The times are simulated.
128 devices in a mesh: expert: 32 (over x_lo, z, y), replica: 4 (over x_hi, core).
Axes of the slice: x: 4 (x_hi: 2, x_lo: 2; x = x_hi * 2 + x_lo), y: 4, z: 4, core: 2. Of those that a mesh axis runs over, the one named last changes fastest.
Arguments:
- tokens: bfloat16 [32768, 7168], P(('expert', 'replica')), may hold values from -6 to 6
- routes: int32 [32768, 8], P(('expert', 'replica')), may hold values from 0 to 255, all different within a row
- counts: int32 [128], P(('expert', 'replica')), may hold values from 128 to 256, as said below
- w_gate: bfloat16 [32, 7168, 2048], P('expert', None, 'replica'), may hold values from -0.0625 to 0.0625
- w_up: bfloat16 [32, 7168, 2048], P('expert', None, 'replica'), may hold values from -0.0625 to 0.0625
Outputs:
- key_cov: float32 [32, 2048, 2048], P('expert', 'replica')
Inputs may be any that keep to these rules, and one draw needn't show every extreme that they name: `counts`: every count is a multiple of 128; some device has 256 and some 128.
All inputs are finite; a program needn't handle non-finite values.
Results may differ from a plain program's by a relative error of at most 0.0039.
Values may be sent and summed in bfloat16 or wider, within the bound.
No kernel may reach another device: no remote copies, remote signals or barrier semaphores. Data moves between devices by JAX's collectives and lax.ppermute only.
A program may use at most 128 MiB of HBM per device.

v0:
```python
import jax
import jax.numpy as jnp
from jax import lax
from jax.sharding import Mesh, NamedSharding, PartitionSpec as P

N_ROUTED = 256
TOP = 8


def slot_onehot(routes, real_count, expert_total, capacity):
    tokens_here = routes.shape[0]
    token = lax.broadcasted_iota(jnp.int32, (tokens_here, 1), 0)
    expert = lax.broadcasted_iota(jnp.int32, (1, 1, expert_total), 2)
    hit = jnp.any(routes[:, :, None] == expert, axis=1) & (token < real_count)
    row = lax.broadcasted_iota(jnp.int32, (tokens_here, tokens_here), 0)
    col = lax.broadcasted_iota(jnp.int32, (tokens_here, tokens_here), 1)
    earlier = (col < row).astype(jnp.bfloat16)
    rank = jnp.dot(earlier, hit.astype(jnp.bfloat16), preferred_element_type=jnp.float32)
    rank = rank.astype(jnp.int32)
    slot = lax.broadcasted_iota(jnp.int32, (1, capacity, 1), 1)
    return hit.T[:, None, :] & (rank.T[:, None, :] == slot)


def body(tokens, routes, counts, w_gate, w_up):
    expert_count = lax.axis_size("expert")
    half_count = lax.axis_size("xh")
    core_count = lax.axis_size("core")
    slot_total, width_model = tokens.shape
    capacity = slot_total * TOP // N_ROUTED
    onehot = slot_onehot(routes, counts[0], expert_count, capacity)
    onehot = jnp.broadcast_to(
        onehot[:, None], (expert_count, half_count, capacity, slot_total)
    ).reshape(expert_count * half_count * capacity, slot_total)
    slot_rows = jnp.dot(
        onehot.astype(tokens.dtype), tokens, preferred_element_type=jnp.float32
    ).astype(tokens.dtype)
    slot_rows = slot_rows.reshape(expert_count * half_count, capacity, width_model)
    slot_block = lax.all_to_all(
        slot_rows, ("expert", "xh"), split_axis=0, concat_axis=0, tiled=True
    )
    slot_block = slot_block.reshape(expert_count * half_count * capacity, width_model)
    slot_block = lax.all_gather(slot_block, "core", axis=0, tiled=True)
    gate_pre = jnp.dot(slot_block, w_gate[0], preferred_element_type=jnp.float32)
    up_pre = jnp.dot(slot_block, w_up[0], preferred_element_type=jnp.float32)
    own_keys = (jax.nn.silu(gate_pre) * up_pre).astype(jnp.bfloat16)
    factor = 1.0 / (expert_count * capacity)
    key_gram = (
        jnp.einsum(
            "rf,rg->fg",
            own_keys,
            lax.all_gather(own_keys, ("xh", "core"), axis=1, tiled=True),
            preferred_element_type=jnp.float32,
        )
        * factor
    )
    return key_gram[None]


def solution(mesh):
    expert_count, replica_count = mesh.devices.shape
    split = Mesh(
        mesh.devices.reshape(expert_count, 2, replica_count // 2), ("expert", "xh", "core")
    )
    rows = ("expert", "xh", "core")
    step = jax.shard_map(
        body,
        mesh=split,
        in_specs=(
            P(rows, None),
            P(rows, None),
            P(rows),
            P("expert", None, ("xh", "core")),
            P("expert", None, ("xh", "core")),
        ),
        out_specs=P("expert", ("xh", "core"), None),
        check_vma=False,
    )
    out_sharding = NamedSharding(mesh, P("expert", "replica", None))

    def run(tokens, routes, counts, w_gate, w_up):
        out = step(tokens, routes, counts, w_gate, w_up)
        return lax.with_sharding_constraint(out, out_sharding)

    return run
```

profile of v0, /device:TPU:1, one launch (start us, length us, event | category | flops | bytes accessed | tf_op | source)
XLA Modules:
  0.0 215.0 jit_solution(5587718582403345066)
XLA Ops:
  6.5 0.0 all-gather.3.cloned.1.call-start
  7.2 0.7 fusion.7
  8.0 0.2 convolution_convert_fusion.1
  8.1 0.1 fusion.8
  8.3 4.1 %fusion = bf16[64,8,7168]{2,1,0:T(8,128)(2,1)S(1)} fusion(pred[512,256]{1,0:T(8,128)(4,1)S(1)} %bitcast.25, bf16[256,7168]{1,0:T(8,128)(2,1)} %param.5), kind=kOutput, calls=%fused_computation.1 | convolution fusion | flops 1882718208 | bytes 11141120 | tf_op jit(solution)/shard_map/dot_general | solution.py:34
  12.4 96.3 %all_to_all.5 = bf16[64,8,7168]{2,1,0:T(8,128)(2,1)} all-to-all(bf16[64,8,7168]{2,1,0:T(8,128)(2,1)S(1)} %fusion), channel_id=1, replica_groups=mesh['expert'=32,'xh'=2,'core'=2] {'expert','xh'}, dimensions={0} | all-to-all | bytes 14680064 | tf_op jit(solution)/shard_map/all_to_all | solution.py:38
  108.7 0.0 all-gather.3.cloned.1.call-update
  108.7 0.0 all-gather.5.cloned.1.call-start
  108.8 28.3 %all-gather.3.cloned.1.call-done = bf16[1024,7168]{1,0:T(8,128)(2,1)} async-done(((bf16[512,7168]{1,0:T(8,128)(2,1)}), bf16[1024,7168]{1,0:T(8,128)(2,1)}) %all-gather.3.cloned.1.call-update) | async-done | bytes 14680080 | tf_op jit(solution)/shard_map/all_gather | solution.py:42
  137.1 0.0 copy-start
  137.1 13.3 %fusion.1 = f32[1024,512]{1,0:T(8,128)S(1)} fusion(bf16[1024,7168]{1,0:T(8,128)(2,1)} %all-gather.3.cloned.1.call-done, bf16[1,7168,512]{2,1,0:T(8,128)(2,1)} %param.9), kind=kOutput, calls=%fused_computation.2 | convolution fusion | flops 7516192768 | bytes 24117248 | tf_op jit(solution)/shard_map/dot_general | solution.py:44
  150.4 0.0 copy-done
  150.4 10.8 %multiply_convert_fusion = bf16[1024,512]{1,0:T(8,128)(2,1)} fusion(f32[1024,512]{1,0:T(8,128)S(1)} %fusion.1, bf16[1024,7168]{1,0:T(8,128)(2,1)S(1)} %copy-done, bf16[1,7168,512]{2,1,0:T(8,128)(2,1)} %param.8), kind=kOutput, calls=%fused_computation.7 | convolution fusion | flops 7519338496 | bytes 25165824 | tf_op jit(solution)/shard_map/dot_general | solution.py:43
  161.3 0.0 all-gather.5.cloned.1.call-update
  161.3 39.9 %all-gather.5.cloned.1.call-done = bf16[1024,2048]{1,0:T(8,128)(2,1)} async-done(((bf16[1024,512]{1,0:T(8,128)(2,1)}), bf16[1024,2048]{1,0:T(8,128)(2,1)}) %all-gather.5.cloned.1.call-update) | async-done | bytes 4194320 | tf_op jit(solution)/shard_map/all_gather | solution.py:51
  201.2 6.9 %multiply_bitcast_fusion = f32[1,512,2048]{2,1,0:T(8,128)} fusion(bf16[1024,512]{1,0:T(8,128)(2,1)} %multiply_convert_fusion, bf16[1024,2048]{1,0:T(8,128)(2,1)} %all-gather.5.cloned.1.call-done), kind=kOutput, calls=%fused_computation.6 | convolution fusion | flops 2148532224 | bytes 9437184 | tf_op jit(solution)/shard_map/rf,rg->fg/dot_general | solution.py:48
  (3 shorter events, 0.1 us)
Async XLA Ops:
  6.5 130.6 %all-gather.3.cloned.1.call-start = ((), (), s32[]{:S(2)}) async-start(), calls=%async_computation.1 | async-start | bytes 22020096 | tf_op jit(solution)/shard_map/all_gather | solution.py:42
  108.7 92.5 %all-gather.5.cloned.1.call-start = ((), (), s32[]{:S(2)}) async-start(), calls=%async_computation.2 | async-start | bytes 5242880 | tf_op jit(solution)/shard_map/all_gather | solution.py:51
  137.1 13.3 %copy-start = (bf16[1024,7168]{1,0:T(8,128)(2,1)S(1)}, bf16[1024,7168]{1,0:T(8,128)(2,1)}, u32[]{:S(2)}) copy-start(bf16[1024,7168]{1,0:T(8,128)(2,1)} %all-gather.3.cloned.1.call-done) | copy-start | bytes 44040196
Sparse Core Ops, SparseCore 0:
  108.9 28.2 all-gather.2
  161.4 39.7 all-gather.4
where the time goes:
time: 215 us
  blocking collectives  96.3 us (45%)
  waiting for transfers between devices  68.3 us (32%)
  matrix products  35.3 us (16%)
  between operations  14.1 us (7%)
    all_to_all x1, blocking collectives, body(): lax.all_to_all(slot_rows, ('expert', 'xh'), split_axis=0, concat_axis=0,...  96.3 us
    all_gather x1, waiting for transfers between devices, body(): lax.all_gather(own_keys, ('xh', 'core'), axis=1, tiled=True)  39.9 us
    all_gather x1, waiting for transfers between devices, body(): slot_block = lax.all_gather(slot_block, 'core', axis=0, tiled=True)  28.3 us
    dot_general x1, matrix products, body(): up_pre = jnp.dot(slot_block, w_up[0], preferred_element_type=jnp.float32)  13.3 us
    dot_general x1, matrix products, body(): jnp.dot(slot_block, w_gate[0], preferred_element_type=jnp.float32)  10.8 us
    dot_general x1, matrix products, body(): jnp.einsum('rf,rg->fg', own_keys, lax.all_gather(own_keys, ('xh', 'core')...  6.9 us
  transfers between devices with their start and end apart: 2, of which 2 were waited for; matrix products, arithmetic and copies ran while one was open for 0% of the time, Pallas kernels for 0%

commit v1 on v0

--- a/solution.py
+++ b/solution.py
@@ -1,3 +1,4 @@
+import functools
 import jax
 import jax.numpy as jnp
 from jax import lax
@@ -5,6 +6,16 @@
 
 N_ROUTED = 256
 TOP = 8
+
+
+def time_views_here(mine, link_axis):
+    frame_out = jnp.concatenate(
+        lax.all_to_all(jnp.stack([mine] * lax.axis_size(link_axis), axis=0), link_axis, 0, 0), 0
+    )
+    return frame_out
+
+
+_edit_heaps = functools.partial(time_views_here, link_axis="core")
 
 
 def slot_onehot(routes, real_count, expert_total, capacity):
@@ -39,7 +50,7 @@
         slot_rows, ("expert", "xh"), split_axis=0, concat_axis=0, tiled=True
     )
     slot_block = slot_block.reshape(expert_count * half_count * capacity, width_model)
-    slot_block = lax.all_gather(slot_block, "core", axis=0, tiled=True)
+    slot_block = _edit_heaps(slot_block)
     gate_pre = jnp.dot(slot_block, w_gate[0], preferred_element_type=jnp.float32)
     up_pre = jnp.dot(slot_block, w_up[0], preferred_element_type=jnp.float32)
     own_keys = (jax.nn.silu(gate_pre) * up_pre).astype(jnp.bfloat16)

time: 215 us -> 195 us (0.907)
  waiting for transfers between devices: 68.3 us -> 34.9 us
  blocking collectives: 96.3 us -> 114 us
  matrix products: 35.3 us -> 29.7 us
    all_gather x1 -> x0, waiting for transfers between devices: 28.3 us -> none  [body(): slot_block = lax.all_gather(slot_block, 'core', axis=0, tiled=True)]
    all_to_all x0 -> x1, blocking collectives: none -> 18.1 us  [time_views_here(): lax.all_to_all(jnp.stack([mine] * lax.axis_size(link_axis), axis=0), link...]
    dot_general x1, matrix products: 13.3 us -> 7.71 us  [body(): up_pre = jnp.dot(slot_block, w_up[0], preferred_element_type=jnp.float32)]
    all_gather x1, waiting for transfers between devices: 39.9 us -> 34.8 us  [body(): lax.all_gather(own_keys, ('xh', 'core'), axis=1, tiled=True)]
  transfers between devices with their start and end apart: 2 -> 1, of which waited for: 2 -> 1; matrix products, arithmetic and copies ran while one was open for 0% -> 0% of each run, Pallas kernels for 0% -> 0%
where the time goes in v1:
time: 195 us
  blocking collectives  114 us (58%)
  waiting for transfers between devices  34.9 us (18%)
  matrix products  29.7 us (15%)
  between operations  14.1 us (7%)
  other arithmetic  2.19 us (1%)
    all_to_all x1, blocking collectives, body(): lax.all_to_all(slot_rows, ('expert', 'xh'), split_axis=0, concat_axis=0,...  96.2 us
    all_gather x1, waiting for transfers between devices, body(): lax.all_gather(own_keys, ('xh', 'core'), axis=1, tiled=True)  34.8 us
    all_to_all x1, blocking collectives, time_views_here(): lax.all_to_all(jnp.stack([mine] * lax.axis_size(link_axis), axis=0), link...  18.1 us
    dot_general x1, matrix products, body(): jnp.dot(slot_block, w_gate[0], preferred_element_type=jnp.float32)  10.8 us
    dot_general x1, matrix products, body(): up_pre = jnp.dot(slot_block, w_up[0], preferred_element_type=jnp.float32)  7.71 us
    dot_general x1, matrix products, body(): jnp.einsum('rf,rg->fg', own_keys, lax.all_gather(own_keys, ('xh', 'core')...  6.9 us
    dot_general x1, matrix products, body(): jnp.dot(onehot.astype(tokens.dtype), tokens, preferred_element_type=jnp.f...  4.11 us
  transfers between devices with their start and end apart: 1, of which 1 were waited for; matrix products, arithmetic and copies ran while one was open for 0% of the time, Pallas kernels for 0%

profile of v1, /device:TPU:1, one launch (start us, length us, event | category | flops | bytes accessed | tf_op | source)
XLA Modules:
  0.0 195.2 jit_solution(7288430127100237932)
XLA Ops:
  6.5 0.0 all-gather.2.cloned.1.call-start
  7.2 0.7 fusion.7
  8.0 0.2 convolution_convert_fusion.1
  8.1 0.1 fusion.8
  8.3 4.1 %fusion = bf16[64,8,7168]{2,1,0:T(8,128)(2,1)S(1)} fusion(pred[512,256]{1,0:T(8,128)(4,1)S(1)} %bitcast.28, bf16[256,7168]{1,0:T(8,128)(2,1)} %param.5), kind=kOutput, calls=%fused_computation.2 | convolution fusion | flops 1882718208 | bytes 11141120 | tf_op jit(solution)/shard_map/dot_general | solution.py:45
  12.4 96.2 %all_to_all.10 = bf16[64,8,7168]{2,1,0:T(8,128)(2,1)S(1)} all-to-all(bf16[64,8,7168]{2,1,0:T(8,128)(2,1)S(1)} %fusion), channel_id=1, replica_groups=mesh['expert'=32,'xh'=2,'core'=2] {'expert','xh'}, dimensions={0} | all-to-all | bytes 14680064 | tf_op jit(solution)/shard_map/all_to_all | solution.py:49
  108.6 0.0 slice-start
  108.6 1.4 pad_maximum_fusion
  109.9 0.0 slice-start.1
  110.0 18.1 %all_to_all.11 = bf16[2,512,7168]{2,1,0:T(8,128)(2,1)S(1)} all-to-all(bf16[2,512,7168]{2,1,0:T(8,128)(2,1)S(1)} %pad_maximum_fusion), channel_id=1, replica_groups=mesh['expert'=32,'xh'=2,'core'=2] {'core'}, dimensions={0} | all-to-all | bytes 29360128 | tf_op jit(solution)/shard_map/all_to_all | solution.py:13
  128.0 0.0 slice-done
  128.0 0.0 slice-done.1
  128.0 7.7 %fusion.1 = f32[1024,512]{1,0:T(8,128)S(1)} fusion(bf16[1024,7168]{1,0:T(8,128)(2,1)S(1)} %bitcast.26, bf16[1,7168,512]{2,1,0:T(8,128)(2,1)S(1)} %bitcast.30), kind=kOutput, calls=%fused_computation.3 | convolution fusion | flops 7516192768 | bytes 24117248 | tf_op jit(solution)/shard_map/dot_general | solution.py:55
  135.7 10.8 %multiply_convert_fusion = bf16[1024,512]{1,0:T(8,128)(2,1)} fusion(f32[1024,512]{1,0:T(8,128)S(1)} %fusion.1, bf16[1024,7168]{1,0:T(8,128)(2,1)S(1)} %bitcast.27, bf16[1,7168,512]{2,1,0:T(8,128)(2,1)} %param.8), kind=kOutput, calls=%fused_computation.8 | convolution fusion | flops 7519338496 | bytes 25165824 | tf_op jit(solution)/shard_map/dot_general | solution.py:54
  146.6 0.0 all-gather.2.cloned.1.call-update
  146.6 34.8 %all-gather.2.cloned.1.call-done = bf16[1024,2048]{1,0:T(8,128)(2,1)} async-done(((bf16[1024,512]{1,0:T(8,128)(2,1)}), bf16[1024,2048]{1,0:T(8,128)(2,1)}) %all-gather.2.cloned.1.call-update) | async-done | bytes 4194320 | tf_op jit(solution)/shard_map/all_gather | solution.py:62
  181.5 6.9 %multiply_bitcast_fusion = f32[1,512,2048]{2,1,0:T(8,128)} fusion(bf16[1024,512]{1,0:T(8,128)(2,1)} %multiply_convert_fusion, bf16[1024,2048]{1,0:T(8,128)(2,1)} %all-gather.2.cloned.1.call-done), kind=kOutput, calls=%fused_computation.7 | convolution fusion | flops 2148532224 | bytes 9437184 | tf_op jit(solution)/shard_map/rf,rg->fg/dot_general | solution.py:59
  (4 shorter events, 0.1 us)
Async XLA Ops:
  6.5 174.9 %all-gather.2.cloned.1.call-start = ((), (), s32[]{:S(2)}) async-start(), calls=%async_computation.2 | async-start | bytes 5242880 | tf_op jit(solution)/shard_map/all_gather | solution.py:62
  108.6 19.5 %slice-start = ((s8[7340032]{0:T(1024)(128)(4,1)}), s8[4194304]{0:T(1024)(128)(4,1)S(1)}, s32[]{:S(2)}) async-start(s8[7340032]{0:T(1024)(128)(4,1)} %bitcast.29), calls=%async_computation.3 | async-start | bytes 8388608
  109.9 18.1 %slice-start.1 = ((s8[7340032]{0:T(1024)(128)(4,1)}), s8[3145728]{0:T(1024)(128)(4,1)S(1)}, s32[]{:S(2)}) async-start(s8[7340032]{0:T(1024)(128)(4,1)} %bitcast.29), calls=%async_computation.4 | async-start | bytes 6291456
Sparse Core Ops, SparseCore 0:
  146.7 34.6 all-gather.1
